TPU v7x, 32 devices: a whole 2x2x4 slice. The times are simulated.
32 devices in a mesh: dp: 4 (over y, x), expert: 8 (over z, core).
Axes of the slice: x: 2, y: 2, z: 4, core: 2. Of those that a mesh axis runs over, the one named last changes fastest.
Arguments:
- tokens: bfloat16 [4096, 2048], P(('dp', 'expert')), may hold values from -6 to 6
- cotangent: bfloat16 [4096, 2048], P(('dp', 'expert')), may hold values from -6 to 6
- expert_ids: int32 [4096, 4], P(('dp', 'expert')), may hold values from 0 to 7, all different within a row; in each aligned block of 128 rows (0 to 127, 128 to 255, ...) at most 96 rows name the same one
- gate_probs: float32 [4096, 4], P(('dp', 'expert')), may hold values from 0.05 to 1
- up_weight: bfloat16 [8, 2048, 768], P('expert', None, 'dp'), may hold values from -0.125 to 0.125
- down_weight: float32 [8, 768, 2048], P('expert', 'dp'), may hold values from -28 to 28
- moment1: float32 [8, 768, 2048], P('expert', 'dp'), may hold values from -60 to 60
- moment2: float32 [8, 768, 2048], P('expert', 'dp'), may hold values from 0.05 to 5
- pair_match: int32 [8], replicated, may hold values from 0 to 7, as said below
Outputs:
- down_out: float32 [8, 768, 2048], P('expert', 'dp')
- moment1_out: float32 [8, 768, 2048], P('expert', 'dp')
- moment2_out: float32 [8, 768, 2048], P('expert', 'dp')
Inputs may be any that keep to these rules, and one draw needn't show every extreme that they name: `expert_ids`: each row names 4 different experts. Within the rows of one device (aligned blocks of 128 rows) no expert is named by more than 96 rows, a bound that some block reaches. A perfect matching: pair_match[pair_match[i]] = i and pair_match[i] != i for every i.
All inputs are finite; a program needn't handle non-finite values.
Results may differ from a plain program's by a relative error of at most 0.00035.
Values may be sent and summed in bfloat16 or wider, within the bound.
No kernel may reach another device: no remote copies, remote signals or barrier semaphores. Data moves between devices by JAX's collectives and lax.ppermute only.
A program may use at most 128 MiB of HBM per device.

v0:
```python
import jax
import jax.numpy as jnp
from jax import lax
from jax.sharding import PartitionSpec as P

beta_one = 0.9
beta_two = 0.999
epsilon = 1e-06
learn_rate = 0.05


def relocate(states, pair_match):
    group_size = lax.axis_size("expert")
    count_states = len(states)
    stacked = jnp.stack(states).reshape(count_states, group_size, -1)
    chosen = jnp.take(
        lax.all_to_all(stacked, "expert", split_axis=1, concat_axis=1, tiled=True),
        pair_match,
        axis=1,
    )
    arrived = lax.all_to_all(chosen, "expert", split_axis=1, concat_axis=1, tiled=True)
    arrived = arrived.reshape((count_states,) + states[0].shape)
    return tuple((arrived[index] for index in range(count_states)))


def expert_gradient(tokens, cotangent, expert_ids, gate_probs, up_weight):
    group_size = lax.axis_size("expert")
    tok_rows, top_count = expert_ids.shape
    width = tokens.shape[1]
    capacity = 3 * tok_rows * top_count // (2 * group_size)
    total = tok_rows * top_count
    flat_ids = expert_ids.reshape(-1)
    picked = (flat_ids[:, None] == jnp.arange(group_size, dtype=jnp.int32)[None, :]).astype(
        jnp.int32
    )
    ranking = jnp.sum((jnp.cumsum(picked, axis=0) - 1) * picked, axis=1)
    slot_index = flat_ids * capacity + ranking
    source = (
        jnp.full((group_size * capacity,), total, jnp.int32)
        .at[slot_index]
        .set(jnp.arange(total, dtype=jnp.int32))
    )
    filled = source < total
    safe_source = jnp.minimum(source, total - 1)
    row_index = safe_source // top_count
    weights_row = jnp.where(filled, gate_probs.reshape(-1)[safe_source], jnp.float32(0.0))
    sent_tokens = jnp.where(filled[:, None], tokens[row_index], jnp.zeros((), jnp.bfloat16))
    sent_scaled = (weights_row[:, None] * cotangent[row_index].astype(jnp.float32)).astype(
        jnp.bfloat16
    )
    sent_tokens = sent_tokens.reshape(group_size, capacity, width)
    sent_scaled = sent_scaled.reshape(group_size, capacity, width)
    got_tokens, got_scaled = (
        lax.all_to_all(sent_tokens, "expert", split_axis=0, concat_axis=0, tiled=True),
        lax.all_to_all(sent_scaled, "expert", split_axis=0, concat_axis=0, tiled=True),
    )
    rows_tokens = got_tokens.reshape(-1, width)
    rows_scaled = got_scaled.reshape(-1, width)
    hidden = jax.nn.silu(
        jnp.dot(
            rows_tokens,
            lax.all_gather(up_weight[0], "dp", axis=1, tiled=True),
            preferred_element_type=jnp.float32,
        )
    ).astype(jnp.bfloat16)
    return lax.psum_scatter(
        lax.dot_general(
            hidden, rows_scaled, (((0,), (0,)), ((), ())), preferred_element_type=jnp.float32
        ),
        "dp",
        scatter_dimension=0,
        tiled=True,
    )


def lamb_step(weight, moment_one, moment_two, gradient):
    first = beta_one * moment_one + (1.0 - beta_one) * gradient
    second = beta_two * moment_two + (1.0 - beta_two) * gradient * gradient
    update = first / (jnp.sqrt(second) + epsilon)
    weight_sq, update_sq = lax.psum((jnp.sum(weight * weight), jnp.sum(update * update)), "dp")
    trust_ratio = jnp.sqrt(weight_sq) / (jnp.sqrt(update_sq) + epsilon)
    renewed = weight - learn_rate * trust_ratio * update
    return (renewed, first, second)


def local(
    tokens, cotangent, expert_ids, gate_probs, up_weight, down_weight, moment1, moment2, pair_match
):
    gradient = expert_gradient(tokens, cotangent, expert_ids, gate_probs, up_weight)
    renewed, first, second = lamb_step(down_weight[0], moment1[0], moment2[0], gradient)
    renewed, first, second = relocate((renewed, first, second), pair_match)
    return (renewed[None], first[None], second[None])


def solution(mesh):
    in_specs = (
        P(("dp", "expert"), None),
        P(("dp", "expert"), None),
        P(("dp", "expert"), None),
        P(("dp", "expert"), None),
        P("expert", None, "dp"),
        P("expert", "dp", None),
        P("expert", "dp", None),
        P("expert", "dp", None),
        P(),
    )
    out_specs = (P("expert", "dp", None), P("expert", "dp", None), P("expert", "dp", None))
    return jax.shard_map(local, mesh=mesh, in_specs=in_specs, out_specs=out_specs, check_vma=False)
```

profile of v0, /device:TPU:0, one launch (start us, length us, event | category | flops | bytes accessed | tf_op | source)
XLA Modules:
  0.0 632.6 jit_solution(5432400970827513326)
XLA Ops:
  14.0 5.0 gather_fusion.1
  19.2 4.3 gather_fusion
  23.5 3.8 broadcast_select_fusion
  27.3 6.5 %all-to-all-start = ((bf16[8,96,2048]{2,1,0:T(8,128)(2,1)}), bf16[8,96,2048]{2,1,0:T(8,128)(2,1)}, u32[]{:S(2)}, u32[]{:S(2)}) async-start(bf16[8,96,2048]{2,1,0:T(8,128)(2,1)} %broadcast_select_fusion), calls=%async_computation | async-start | bytes 6291456 | tf_op jit(solution)/shard_map/all_to_all | solution.py:54
  33.9 4.2 gather_fusion.2
  38.1 4.2 fusion
  42.3 63.1 %all-to-all-done = bf16[8,96,2048]{2,1,0:T(8,128)(2,1)} async-done(((bf16[8,96,2048]{2,1,0:T(8,128)(2,1)}), bf16[8,96,2048]{2,1,0:T(8,128)(2,1)}, u32[]{:S(2)}, u32[]{:S(2)}) %all-to-all-start) | async-done | bytes 3145760 | tf_op jit(solution)/shard_map/all_to_all | solution.py:54
  105.4 4.4 all-to-all-start.1
  110.8 46.9 %all-gather.3.cloned.1.call-done = bf16[1,2048,768]{1,2,0:T(8,128)(2,1)} async-done(((bf16[1,2048,192]{1,2,0:T(8,128)(2,1)}), bf16[1,2048,768]{1,2,0:T(8,128)(2,1)}) %all-gather.3.cloned.1.call-update) | async-done | bytes 3145744 | tf_op jit(solution)/shard_map/all_gather | solution.py:62
  157.7 23.6 %all-to-all-done.1 = bf16[8,96,2048]{2,1,0:T(8,128)(2,1)} async-done(((bf16[8,96,2048]{2,1,0:T(8,128)(2,1)}), bf16[8,96,2048]{2,1,0:T(8,128)(2,1)}, u32[]{:S(2)}, u32[]{:S(2)}) %all-to-all-start.1) | async-done | bytes 3145760 | tf_op jit(solution)/shard_map/all_to_all | solution.py:55
  181.3 16.3 %fusion.8 = f32[768,2048]{1,0:T(8,128)} fusion(bf16[768,2048]{1,0:T(8,128)(2,1)} %bitcast.10, bf16[768,2048]{1,0:T(8,128)(2,1)} %bitcast.7, bf16[1,2048,768]{1,2,0:T(8,128)(2,1)} %all-gather.3.cloned.1.call-done), kind=kOutput, calls=%fused_computation.24 | convolution fusion | flops 4834787328 | bytes 15728640 | tf_op jit(solution)/shard_map/dot_general | solution.py:67
  200.0 66.7 %reduce-scatter.2.cloned.1.call-done = f32[192,2048]{1,0:T(8,128)} async-done(((f32[768,2048]{1,0:T(8,128)}), f32[192,2048]{1,0:T(8,128)}) %reduce-scatter.2.cloned.1.call-update) | async-done | bytes 1572880 | tf_op jit(solution)/shard_map/reduce_scatter | solution.py:66
  266.8 5.0 multiply_reduce_fusion
  271.8 9.8 %all-reduce = (f32[]{:T(128)}, f32[]{:T(128)}) all-reduce(f32[]{:T(128)} %fusion.6, f32[]{:T(128)} %get-tuple-element.8), channel_id=1, replica_groups=mesh['dp'=4,'expert'=8] {'dp'}, use_global_device_ids=true, to_apply=%region_1.2 | all-reduce | flops 2 | bytes 16 | tf_op jit(solution)/shard_map/psum | solution.py:80
  285.7 4.2 stack.18
  290.0 3.7 bitcast_subtract_fusion
  293.7 4.4 stack.16
  298.0 7.5 %pad_maximum_fusion = f32[3,8,49152]{2,0,1:T(4,128)} fusion(f32[1,8,49152]{2,0,1:T(1,128)} %stack.18, f32[1,8,49152]{2,0,1:T(1,128)S(1)} %copy-done.4, f32[1,8,49152]{2,0,1:T(1,128)} %stack.16), kind=kLoop, calls=%fused_computation.5 | loop fusion | flops 2359296 | bytes 9437184 | tf_op jit(solution)/shard_map/stack | solution.py:15
  305.5 4.9 all-to-all-start.2
  310.5 138.9 %all-to-all-done.2 = f32[3,8,49152]{2,0,1:T(4,128)} async-done(((f32[3,8,49152]{2,0,1:T(4,128)}), f32[3,8,49152]{2,0,1:T(4,128)}, u32[]{:S(2)}, u32[]{:S(2)}) %all-to-all-start.2) | async-done | bytes 4718624 | tf_op jit(solution)/shard_map/all_to_all | solution.py:17
  449.3 9.4 %gather_fusion.3 = f32[8,3,49152]{2,1,0:T(4,128)} fusion(f32[3,8,49152]{2,0,1:T(4,128)} %all-to-all-done.2, s32[1024]{0:T(1024)S(1)} %pad_clamp_fusion), kind=kCustom, calls=%fused_computation.3 | custom fusion | bytes 9437216 | tf_op jit(solution)/shard_map/jit(_take)/gather | solution.py:16
  458.7 4.4 select_bitcast_fusion
  463.1 141.4 %all_to_all.20 = f32[3,8,49152]{2,0,1:T(4,128)S(1)} all-to-all(f32[3,8,49152]{2,0,1:T(4,128)S(1)} %select_bitcast_fusion), channel_id=1, replica_groups=mesh['dp'=4,'expert'=8] {'expert'}, dimensions={1} | all-to-all | bytes 9437184 | tf_op jit(solution)/shard_map/all_to_all | solution.py:21
  604.5 14.1 %slice_reduce_fusion = (f32[8,49152]{1,0:T(8,128)S(1)}, f32[8,49152]{1,0:T(8,128)}, f32[8,49152]{1,0:T(8,128)}) fusion(f32[3,8,49152]{2,0,1:T(4,128)S(1)} %all_to_all.20), kind=kLoop, calls=%fused_computation.15 | loop fusion | bytes 9437184 | tf_op jit(solution)/shard_map/slice | solution.py:23
  (46 shorter events, 20.2 us)
Async XLA Ops:
  7.2 12.0 %copy-start = (bf16[128,2048]{1,0:T(8,128)(2,1)S(1)}, bf16[128,2048]{1,0:T(8,128)(2,1)}, u32[]{:S(2)}) copy-start(bf16[128,2048]{1,0:T(8,128)(2,1)} %param.9) | copy-start | bytes 1572868
  27.3 6.6 %copy-start.2 = (bf16[128,2048]{1,0:T(8,128)(2,1)S(1)}, bf16[128,2048]{1,0:T(8,128)(2,1)}, u32[]{:S(2)}) copy-start(bf16[128,2048]{1,0:T(8,128)(2,1)} %param.10) | copy-start | bytes 1572868
  27.3 78.1 %all-to-all-start = ((bf16[8,96,2048]{2,1,0:T(8,128)(2,1)}), bf16[8,96,2048]{2,1,0:T(8,128)(2,1)}, u32[]{:S(2)}, u32[]{:S(2)}) async-start(bf16[8,96,2048]{2,1,0:T(8,128)(2,1)} %broadcast_select_fusion), calls=%async_computation | async-start | bytes 6291456 | tf_op jit(solution)/shard_map/all_to_all | solution.py:54
  105.4 76.0 %all-to-all-start.1 = ((bf16[8,96,2048]{2,1,0:T(8,128)(2,1)}), bf16[8,96,2048]{2,1,0:T(8,128)(2,1)}, u32[]{:S(2)}, u32[]{:S(2)}) async-start(bf16[8,96,2048]{2,1,0:T(8,128)(2,1)} %fusion), calls=%async_computation.1 | async-start | bytes 6291456 | tf_op jit(solution)/shard_map/all_to_all | solution.py:55
  109.8 47.9 %all-gather.3.cloned.1.call-start = ((), (), s32[]{:S(2)}) async-start(), calls=%async_computation.6 | async-start | bytes 3932160 | tf_op jit(solution)/shard_map/all_gather | solution.py:62
  110.6 156.2 %reduce-scatter.2.cloned.1.call-start = ((), (), s32[]{:S(2)}) async-start(), calls=%async_computation.5 | async-start | bytes 7864320 | tf_op jit(solution)/shard_map/reduce_scatter | solution.py:66
  197.6 1.4 copy-start.3
  293.7 4.4 copy-start.4
  305.5 4.9 copy-start.5
  305.5 143.8 %all-to-all-start.2 = ((f32[3,8,49152]{2,0,1:T(4,128)}), f32[3,8,49152]{2,0,1:T(4,128)}, u32[]{:S(2)}, u32[]{:S(2)}) async-start(f32[3,8,49152]{2,0,1:T(4,128)} %pad_maximum_fusion), calls=%async_computation.3 | async-start | bytes 12582912 | tf_op jit(solution)/shard_map/all_to_all | solution.py:17
  624.3 1.4 copy-start.1
Sparse Core Ops, SparseCore 0:
  112.5 45.1 all-gather.2
  197.8 68.9 reduce-scatter.1
where the time goes:
time: 633 us
  waiting for transfers between devices  340 us (54%)
  blocking collectives  151 us (24%)
  local copies, waits for them, and re-layouts  61.9 us (10%)
  other arithmetic  31.6 us (5%)
  matrix products  16.3 us (3%)
  starting transfers between devices  16.1 us (3%)
  between operations  15.6 us (2%)
    all_to_all x1, blocking collectives, relocate(): lax.all_to_all(chosen, 'expert', split_axis=1, concat_axis=1, tiled=True)  141 us
    all_to_all x1, waiting for transfers between devices, relocate(): lax.all_to_all(stacked, 'expert', split_axis=1, concat_axis=1, tiled=True)  139 us
    reduce_scatter x1, waiting for transfers between devices, expert_gradient(): lax.psum_scatter(lax.dot_general(hidden, rows_scaled, (((0,), (0,)), ((),...  66.7 us
    all_to_all x1, waiting for transfers between devices, expert_gradient(): lax.all_to_all(sent_tokens, 'expert', split_axis=0, concat_axis=0, tiled=...  63.1 us
    all_gather x1, waiting for transfers between devices, expert_gradient(): lax.all_gather(up_weight[0], 'dp', axis=1, tiled=True)  46.9 us
    all_to_all x1, waiting for transfers between devices, expert_gradient(): lax.all_to_all(sent_scaled, 'expert', split_axis=0, concat_axis=0, tiled=...  23.6 us
    slice x4, local copies, waits for them, and re-layouts, relocate(): return tuple((arrived[index] for index in range(count_states)))  21.2 us
    dot_general x1, matrix products, expert_gradient(): lax.dot_general(hidden, rows_scaled, (((0,), (0,)), ((), ())), preferred_...  16.3 us
  transfers between devices with their start and end apart: 5, of which 5 were waited for; matrix products, arithmetic and copies ran while one was open for 1% of the time, Pallas kernels for 0%

commit v1 on v0

--- a/solution.py
+++ b/solution.py
@@ -7,6 +7,8 @@
 beta_two = 0.999
 epsilon = 1e-06
 learn_rate = 0.05
+
+dense_rows_max = 2048
 
 
 def relocate(states, pair_match):
@@ -23,13 +25,13 @@
     return tuple((arrived[index] for index in range(count_states)))
 
 
-def expert_gradient(tokens, cotangent, expert_ids, gate_probs, up_weight):
+def routed_gradient(tokens, cotangent, dest_ids, gate_probs, up_full):
     group_size = lax.axis_size("expert")
-    tok_rows, top_count = expert_ids.shape
+    tok_rows, top_count = dest_ids.shape
     width = tokens.shape[1]
     capacity = 3 * tok_rows * top_count // (2 * group_size)
     total = tok_rows * top_count
-    flat_ids = expert_ids.reshape(-1)
+    flat_ids = dest_ids.reshape(-1)
     picked = (flat_ids[:, None] == jnp.arange(group_size, dtype=jnp.int32)[None, :]).astype(
         jnp.int32
     )
@@ -57,19 +59,25 @@
     rows_tokens = got_tokens.reshape(-1, width)
     rows_scaled = got_scaled.reshape(-1, width)
     hidden = jax.nn.silu(
-        jnp.dot(
-            rows_tokens,
-            lax.all_gather(up_weight[0], "dp", axis=1, tiled=True),
-            preferred_element_type=jnp.float32,
-        )
+        jnp.dot(rows_tokens, up_full, preferred_element_type=jnp.float32)
     ).astype(jnp.bfloat16)
-    return lax.psum_scatter(
-        lax.dot_general(
-            hidden, rows_scaled, (((0,), (0,)), ((), ())), preferred_element_type=jnp.float32
-        ),
-        "dp",
-        scatter_dimension=0,
-        tiled=True,
+    return lax.dot_general(
+        hidden, rows_scaled, (((0,), (0,)), ((), ())), preferred_element_type=jnp.float32
+    )
+
+
+def dense_gradient(tokens, cotangent, expert_ids, gate_probs, up_full, expert):
+    all_tokens = lax.all_gather(tokens, "expert", axis=0, tiled=True)
+    all_cot = lax.all_gather(cotangent, "expert", axis=0, tiled=True)
+    all_ids = lax.all_gather(expert_ids, "expert", axis=0, tiled=True)
+    all_gates = lax.all_gather(gate_probs, "expert", axis=0, tiled=True)
+    weights_row = jnp.sum(jnp.where(all_ids == expert, all_gates, jnp.float32(0.0)), axis=1)
+    scaled = (weights_row[:, None] * all_cot.astype(jnp.float32)).astype(jnp.bfloat16)
+    hidden = jax.nn.silu(
+        jnp.dot(all_tokens, up_full, preferred_element_type=jnp.float32)
+    ).astype(jnp.bfloat16)
+    return lax.dot_general(
+        hidden, scaled, (((0,), (0,)), ((), ())), preferred_element_type=jnp.float32
     )
 
 
@@ -86,9 +94,17 @@
 def local(
     tokens, cotangent, expert_ids, gate_probs, up_weight, down_weight, moment1, moment2, pair_match
 ):
-    gradient = expert_gradient(tokens, cotangent, expert_ids, gate_probs, up_weight)
-    renewed, first, second = lamb_step(down_weight[0], moment1[0], moment2[0], gradient)
-    renewed, first, second = relocate((renewed, first, second), pair_match)
+    group_size = lax.axis_size("expert")
+    partner = pair_match[lax.axis_index("expert")]
+    weight, moment_one, moment_two = relocate((down_weight[0], moment1[0], moment2[0]), pair_match)
+    (up_local,) = relocate((up_weight[0],), pair_match)
+    up_full = lax.all_gather(up_local, "dp", axis=1, tiled=True)
+    if group_size * tokens.shape[0] <= dense_rows_max:
+        partial = dense_gradient(tokens, cotangent, expert_ids, gate_probs, up_full, partner)
+    else:
+        partial = routed_gradient(tokens, cotangent, pair_match[expert_ids], gate_probs, up_full)
+    gradient = lax.psum_scatter(partial, "dp", scatter_dimension=0, tiled=True)
+    renewed, first, second = lamb_step(weight, moment_one, moment_two, gradient)
     return (renewed[None], first[None], second[None])
 
 

time: 633 us -> 513 us (0.81)
  waiting for transfers between devices: 340 us -> 64.5 us
  blocking collectives: 151 us -> 307 us
  local copies, waits for them, and re-layouts: 61.9 us -> 46.4 us
  other arithmetic: 31.6 us -> 43.6 us
    all_gather x0 -> x2, blocking collectives: none -> 155 us  [the longest x1 142 us: dense_gradient(): all_ids = lax.all_gather(expert_ids, 'expert', axis=0, tiled=True)]
    all_to_all x1 -> x2, waiting for transfers between devices: 139 us -> 41.7 us  [relocate(): lax.all_to_all(stacked, 'expert', split_axis=1, concat_axis=1, tiled=True)]
    reduce_scatter x1, waiting for transfers between devices: 66.7 us -> 0.02 us  [local(): gradient = lax.psum_scatter(partial, 'dp', scatter_dimension=0, tiled=True)]
    all_to_all x2 -> x1, waiting for transfers between devices: 86.8 us -> 21.5 us  [relocate(): lax.all_to_all(chosen, 'expert', split_axis=1, concat_axis=1, tiled=True)]
    all_gather x1 -> x3, waiting for transfers between devices: 46.9 us -> 0.06 us  [the longest x1 0.02 us: dense_gradient(): all_tokens = lax.all_gather(tokens, 'expert', axis=0, tiled=True)]
    slice x5 -> x0, local copies, waits for them, and re-layouts: 21.4 us -> none  [the longest x4 21.2 us: relocate(): return tuple((arrived[index] for index in range(count_states)))]
    reduce_sum x1, other arithmetic: 1 us -> 15.8 us  [lamb_step(): jnp.sum(weight * weight)]
    reshape x1 -> x2, local copies, waits for them, and re-layouts: 0.1 us -> 13.9 us  [relocate(): stacked = jnp.stack(states).reshape(count_states, group_size, -1)]
  transfers between devices with their start and end apart: 5 -> 7, of which waited for: 5 -> 2; matrix products, arithmetic and copies ran while one was open for 1% -> 19% of each run, Pallas kernels for 0% -> 0%
where the time goes in v1:
time: 513 us; the launch traced here: 507 us
  blocking collectives  307 us (60%)
  waiting for transfers between devices  64.5 us (13%)
  local copies, waits for them, and re-layouts  46.4 us (9%)
  other arithmetic  43.6 us (8%)
  between operations  15.6 us (3%)
  starting transfers between devices  15.4 us (3%)
  matrix products  14 us (3%)
    all_gather x1, blocking collectives, dense_gradient(): all_ids = lax.all_gather(expert_ids, 'expert', axis=0, tiled=True)  142 us
    all_to_all x1, blocking collectives, relocate(): lax.all_to_all(chosen, 'expert', split_axis=1, concat_axis=1, tiled=True)  142 us
    all_to_all x2, waiting for transfers between devices, relocate(): lax.all_to_all(stacked, 'expert', split_axis=1, concat_axis=1, tiled=True)  41.7 us
    all_to_all x1, waiting for transfers between devices, relocate(): lax.all_to_all(chosen, 'expert', split_axis=1, concat_axis=1, tiled=True)  21.5 us
    reduce_sum x1, other arithmetic, lamb_step(): jnp.sum(weight * weight)  15.8 us
    dot_general x1, matrix products, dense_gradient(): lax.dot_general(hidden, scaled, (((0,), (0,)), ((), ())), preferred_eleme...  14 us
    reshape x2, local copies, waits for them, and re-layouts, relocate(): stacked = jnp.stack(states).reshape(count_states, group_size, -1)  13.9 us
    all_gather x1, blocking collectives, dense_gradient(): all_gates = lax.all_gather(gate_probs, 'expert', axis=0, tiled=True)  12.9 us
  transfers between devices with their start and end apart: 7, of which 2 were waited for; matrix products, arithmetic and copies ran while one was open for 19% of the time, Pallas kernels for 0%

profile of v1, /device:TPU:0, one launch (start us, length us, event | category | flops | bytes accessed | tf_op | source)
XLA Modules:
  0.0 507.1 jit_solution(3654276904024603377)
XLA Ops:
  7.9 1.4 copy.22
  11.3 5.4 %reduce.9 = bf16[8,49152]{1,0:T(8,128)(2,1)S(1)} reduce(bf16[8,1,49152]{2,1,0:T(2,128)(2,1)S(1)} %bitcast.39, bf16[]{:T(256)} %broadcast.65), dimensions={1}, to_apply=%bitcast.28.reduce_sub_computation | reduce | bytes 1572866
  16.7 1.5 reshape.75
  18.2 6.4 %all-to-all-start.2 = ((bf16[8,2,24576]{2,1,0:T(2,128)(2,1)}), bf16[8,2,24576]{2,1,0:T(2,128)(2,1)S(1)}, u32[]{:S(2)}, u32[]{:S(2)}) async-start(bf16[8,2,24576]{2,1,0:T(2,128)(2,1)} %reshape.75), calls=%async_computation.2 | async-start | bytes 1572864 | tf_op jit(solution)/shard_map/all_to_all | solution.py:19
  25.4 41.7 %all-to-all-done.2 = bf16[8,2,24576]{2,1,0:T(2,128)(2,1)S(1)} async-done(((bf16[8,2,24576]{2,1,0:T(2,128)(2,1)}), bf16[8,2,24576]{2,1,0:T(2,128)(2,1)S(1)}, u32[]{:S(2)}, u32[]{:S(2)}) %all-to-all-start.2) | async-done | bytes 786464 | tf_op jit(solution)/shard_map/all_to_all | solution.py:19
  71.2 5.4 %reduce.10 = bf16[8,49152]{1,0:T(8,128)(2,1)S(1)} reduce(bf16[8,1,49152]{2,1,0:T(2,128)(2,1)S(1)} %bitcast.40, bf16[]{:T(256)} %broadcast.65), dimensions={1}, to_apply=%bitcast.37.reduce_sub_computation | reduce | bytes 1572866
  76.7 1.5 reshape.77
  78.2 4.0 all-to-all-start.3
  82.1 4.7 pad_maximum_fusion
  86.9 5.7 %reshape.50 = f32[3,8,49152]{2,1,0:T(8,128)} reshape(f32[3,192,2048]{2,1,0:T(8,128)} %pad_maximum_fusion) | data formatting | bytes 9437184 | tf_op jit(solution)/shard_map/reshape | solution.py:17
  92.6 8.2 %copy.21 = f32[3,8,49152]{2,0,1:T(4,128)} copy(f32[3,8,49152]{2,1,0:T(8,128)} %reshape.50) | data formatting | bytes 9437184 | tf_op jit(solution)/shard_map/reshape | solution.py:17
  100.8 21.5 %all-to-all-done.3 = bf16[8,2,24576]{2,1,0:T(2,128)(2,1)S(1)} async-done(((bf16[8,2,24576]{2,1,0:T(2,128)(2,1)}), bf16[8,2,24576]{2,1,0:T(2,128)(2,1)S(1)}, u32[]{:S(2)}, u32[]{:S(2)}) %all-to-all-start.3) | async-done | bytes 786464 | tf_op jit(solution)/shard_map/all_to_all | solution.py:23
  122.3 4.8 all-to-all-start
  127.9 4.5 bitcast_reduce_fusion
  135.6 142.2 %all_gather.17 = s32[1024,4]{0,1:T(4,128)S(1)} all-gather(s32[128,4]{0,1:T(4,128)S(1)} %copy-done.1), channel_id=1, replica_groups=mesh['dp'=4,'expert'=8] {'expert'}, dimensions={0}, use_global_device_ids=true | all-gather | bytes 18432 | tf_op jit(solution)/shard_map/all_gather | solution.py:72
  277.7 12.9 %all_gather.18 = f32[1024,4]{0,1:T(4,128)S(1)} all-gather(f32[128,4]{0,1:T(4,128)S(1)} %copy-done.2), channel_id=1, replica_groups=mesh['dp'=4,'expert'=8] {'expert'}, dimensions={0}, use_global_device_ids=true | all-gather | bytes 18432 | tf_op jit(solution)/shard_map/all_gather | solution.py:73
  291.4 14.0 %fusion = f32[768,2048]{1,0:T(8,128)} fusion(bf16[1024,2048]{1,0:T(8,128)(2,1)} %all-gather.8.cloned.1.call-done, f32[1024]{0:T(1024)S(1)} %select_reduce_fusion, bf16[2048,768]{0,1:T(8,128)(2,1)} %all-gather.4.cloned.1.call-done, bf16[1024,2048]{1,0:T(8,128)(2,1)} %all-gather.6.cloned.1.call-done), kind=kOutput, calls=%fused_computation.5 | convolution fusion | flops 6452674560 | bytes 17829888 | tf_op jit(solution)/shard_map/dot_general | solution.py:79
  305.5 9.3 %gather_fusion = f32[8,3,49152]{2,1,0:T(4,128)} fusion(f32[3,8,49152]{2,0,1:T(4,128)} %all-to-all-done, s32[1024]{0:T(1024)S(1)} %pad_clamp_fusion), kind=kCustom, calls=%fused_computation | custom fusion | bytes 9437216 | tf_op jit(solution)/shard_map/jit(_take)/gather | solution.py:18
  314.8 4.4 select_bitcast_fusion
  319.2 141.9 %all_to_all.20 = f32[3,8,49152]{2,0,1:T(4,128)S(1)} all-to-all(f32[3,8,49152]{2,0,1:T(4,128)S(1)} %select_bitcast_fusion), channel_id=1, replica_groups=mesh['dp'=4,'expert'=8] {'expert'}, dimensions={1} | all-to-all | bytes 9437184 | tf_op jit(solution)/shard_map/all_to_all | solution.py:23
  461.1 15.8 %multiply_reduce_fusion.1 = (f32[]{:T(128)}, f32[8,49152]{1,0:T(8,128)}, f32[8,49152]{1,0:T(8,128)S(1)}, f32[8,49152]{1,0:T(8,128)S(1)}) fusion(f32[3,8,49152]{2,0,1:T(4,128)S(1)} %all_to_all.20), kind=kLoop, calls=%fused_computation.23 | loop fusion | flops 1572863 | bytes 9437188 | tf_op jit(solution)/shard_map/reduce_sum | solution.py:88
  476.9 2.8 mul.69
  481.5 5.6 %multiply_reduce_fusion = (f32[]{:T(128)}, f32[192,2048]{1,0:T(8,128)S(1)}, f32[1,192,2048]{2,1,0:T(8,128)}, f32[1,192,2048]{2,1,0:T(8,128)}) fusion(f32[192,2048]{1,0:T(8,128)} %mul.69, f32[192,2048]{1,0:T(8,128)} %reduce-scatter.2.cloned.1.call-done, f32[192,2048]{1,0:T(8,128)} %mul.61), kind=kLoop, calls=%fused_computation.20 | loop fusion | flops 3538943 | bytes 9437188 | tf_op jit(solution)/shard_map/reduce_sum | solution.py:88
  487.2 10.5 %all-reduce = (f32[]{:T(128)}, f32[]{:T(128)}) all-reduce(f32[]{:T(128)} %get-tuple-element.3, f32[]{:T(128)} %get-tuple-element.9), channel_id=1, replica_groups=mesh['dp'=4,'expert'=8] {'dp'}, use_global_device_ids=true, to_apply=%region_1.2 | all-reduce | flops 2 | bytes 16 | tf_op jit(solution)/shard_map/psum | solution.py:88
  (39 shorter events, 15.2 us)
Async XLA Ops:
  7.2 284.2 %all-gather.6.cloned.1.call-start = ((), (), s32[]{:S(2)}) async-start(), calls=%async_computation.6 | async-start | bytes 4718592 | tf_op jit(solution)/shard_map/all_gather | solution.py:70
  16.7 8.6 %copy-start.3 = (s32[8]{0:T(128)S(1)}, s32[8]{0:T(128)}, u32[]{:S(2)}) copy-start(s32[8]{0:T(128)} %param.17) | copy-start | bytes 100
  18.2 48.9 %all-to-all-start.2 = ((bf16[8,2,24576]{2,1,0:T(2,128)(2,1)}), bf16[8,2,24576]{2,1,0:T(2,128)(2,1)S(1)}, u32[]{:S(2)}, u32[]{:S(2)}) async-start(bf16[8,2,24576]{2,1,0:T(2,128)(2,1)} %reshape.75), calls=%async_computation.2 | async-start | bytes 1572864 | tf_op jit(solution)/shard_map/all_to_all | solution.py:19
  24.6 266.8 %all-gather.8.cloned.1.call-start = ((), (), s32[]{:S(2)}) async-start(), calls=%async_computation.7 | async-start | bytes 4718592 | tf_op jit(solution)/shard_map/all_gather | solution.py:71
  76.6 5.5 %copy-start = (f32[1,192,2048]{2,1,0:T(8,128)S(1)}, f32[1,192,2048]{2,1,0:T(8,128)}, u32[]{:S(2)}) copy-start(f32[1,192,2048]{2,1,0:T(8,128)} %param.16) | copy-start | bytes 4718596
  78.2 44.1 %all-to-all-start.3 = ((bf16[8,2,24576]{2,1,0:T(2,128)(2,1)}), bf16[8,2,24576]{2,1,0:T(2,128)(2,1)S(1)}, u32[]{:S(2)}, u32[]{:S(2)}) async-start(bf16[8,2,24576]{2,1,0:T(2,128)(2,1)} %reshape.77), calls=%async_computation.3 | async-start | bytes 1572864 | tf_op jit(solution)/shard_map/all_to_all | solution.py:23
  122.3 183.2 %all-to-all-start = ((f32[3,8,49152]{2,0,1:T(4,128)}), f32[3,8,49152]{2,0,1:T(4,128)}, u32[]{:S(2)}, u32[]{:S(2)}) async-start(f32[3,8,49152]{2,0,1:T(4,128)} %copy.21), calls=%async_computation | async-start | bytes 12582912 | tf_op jit(solution)/shard_map/all_to_all | solution.py:19
  127.1 164.3 %all-gather.4.cloned.1.call-start = ((), (), s32[]{:S(2)}) async-start(), calls=%async_computation.5 | async-start | bytes 3932160 | tf_op jit(solution)/shard_map/all_gather | solution.py:101
  133.6 1.9 copy-start.1
  133.6 144.1 %copy-start.2 = (f32[128,4]{0,1:T(4,128)S(1)}, f32[128,4]{0,1:T(4,128)}, u32[]{:S(2)}) copy-start(f32[128,4]{0,1:T(4,128)} %param.12) | copy-start | bytes 6148
  134.9 346.6 %reduce-scatter.2.cloned.1.call-start = ((), (), s32[]{:S(2)}) async-start(), calls=%async_computation.8 | async-start | bytes 7864320 | tf_op jit(solution)/shard_map/reduce_scatter | solution.py:106
Sparse Core Ops, SparseCore 0:
  9.6 66.4 all-gather.5
  77.6 73.1 all-gather.7
  153.2 57.2 all-gather.3
  305.6 68.6 reduce-scatter.1

commit v2 on v1

--- a/solution.py
+++ b/solution.py
@@ -11,18 +11,13 @@
 dense_rows_max = 2048
 
 
-def relocate(states, pair_match):
+def relocate(state, pair_match):
     group_size = lax.axis_size("expert")
-    count_states = len(states)
-    stacked = jnp.stack(states).reshape(count_states, group_size, -1)
-    chosen = jnp.take(
-        lax.all_to_all(stacked, "expert", split_axis=1, concat_axis=1, tiled=True),
-        pair_match,
-        axis=1,
-    )
-    arrived = lax.all_to_all(chosen, "expert", split_axis=1, concat_axis=1, tiled=True)
-    arrived = arrived.reshape((count_states,) + states[0].shape)
-    return tuple((arrived[index] for index in range(count_states)))
+    pieces = state.reshape((group_size, -1) + state.shape[1:])
+    spread = lax.all_to_all(pieces, "expert", split_axis=0, concat_axis=0, tiled=True)
+    chosen = jnp.take(spread, pair_match, axis=0)
+    arrived = lax.all_to_all(chosen, "expert", split_axis=0, concat_axis=0, tiled=True)
+    return arrived.reshape(state.shape)
 
 
 def routed_gradient(tokens, cotangent, dest_ids, gate_probs, up_full):
@@ -67,14 +62,16 @@
 
 
 def dense_gradient(tokens, cotangent, expert_ids, gate_probs, up_full, expert):
-    all_tokens = lax.all_gather(tokens, "expert", axis=0, tiled=True)
-    all_cot = lax.all_gather(cotangent, "expert", axis=0, tiled=True)
-    all_ids = lax.all_gather(expert_ids, "expert", axis=0, tiled=True)
-    all_gates = lax.all_gather(gate_probs, "expert", axis=0, tiled=True)
-    weights_row = jnp.sum(jnp.where(all_ids == expert, all_gates, jnp.float32(0.0)), axis=1)
-    scaled = (weights_row[:, None] * all_cot.astype(jnp.float32)).astype(jnp.bfloat16)
+    top_count = expert_ids.shape[1]
+    rows = lax.all_gather(jnp.stack((tokens, cotangent)), "expert", axis=1, tiled=True)
+    routing = jnp.concatenate((gate_probs, expert_ids.astype(jnp.float32)), axis=1)
+    routing = lax.all_gather(routing, "expert", axis=0, tiled=True)
+    all_gates, all_ids = routing[:, :top_count], routing[:, top_count:]
+    chosen = all_ids == expert.astype(jnp.float32)
+    weights_row = jnp.sum(jnp.where(chosen, all_gates, jnp.float32(0.0)), axis=1)
+    scaled = (weights_row[:, None] * rows[1].astype(jnp.float32)).astype(jnp.bfloat16)
     hidden = jax.nn.silu(
-        jnp.dot(all_tokens, up_full, preferred_element_type=jnp.float32)
+        jnp.dot(rows[0], up_full, preferred_element_type=jnp.float32)
     ).astype(jnp.bfloat16)
     return lax.dot_general(
         hidden, scaled, (((0,), (0,)), ((), ())), preferred_element_type=jnp.float32
@@ -96,8 +93,10 @@
 ):
     group_size = lax.axis_size("expert")
     partner = pair_match[lax.axis_index("expert")]
-    weight, moment_one, moment_two = relocate((down_weight[0], moment1[0], moment2[0]), pair_match)
-    (up_local,) = relocate((up_weight[0],), pair_match)
+    up_local = relocate(up_weight[0], pair_match)
+    weight = relocate(down_weight[0], pair_match)
+    moment_one = relocate(moment1[0], pair_match)
+    moment_two = relocate(moment2[0], pair_match)
     up_full = lax.all_gather(up_local, "dp", axis=1, tiled=True)
     if group_size * tokens.shape[0] <= dense_rows_max:
         partial = dense_gradient(tokens, cotangent, expert_ids, gate_probs, up_full, partner)

time: 513 us -> 436 us (0.85); the launches traced: 507 us -> 435 us
  blocking collectives: 307 us -> 239 us
  waiting for transfers between devices: 64.5 us -> 113 us
  local copies, waits for them, and re-layouts: 46.4 us -> 13.1 us
  other arithmetic: 43.6 us -> 16.2 us
  matrix products: 14 us -> 20.1 us
    all_gather x2 -> x1, blocking collectives: 155 us -> 83.7 us  [dense_gradient(): routing = lax.all_gather(routing, 'expert', axis=0, tiled=True)]
    all_to_all x3 -> x4, waiting for transfers between devices: 63.2 us -> 90.9 us  [the longest x3 55.9 us: relocate(): lax.all_to_all(pieces, 'expert', split_axis=0, concat_axis=0, tiled=True)]
    all_gather x2 -> x1, waiting for transfers between devices: 0.04 us -> 22 us  [dense_gradient(): lax.all_gather(jnp.stack((tokens, cotangent)), 'expert', axis=1, tiled=True)]
    reduce_sum x1, other arithmetic: 15.8 us -> 1.06 us  [lamb_step(): jnp.sum(weight * weight)]
    reshape x2 -> x1, local copies, waits for them, and re-layouts: 13.9 us -> 0.97 us  [relocate(): return arrived.reshape(state.shape)]
    unnamed x2 -> x0, other arithmetic: 10.9 us -> none
    dot_general x1, matrix products: 14 us -> 20.1 us  [dense_gradient(): lax.dot_general(hidden, scaled, (((0,), (0,)), ((), ())), preferred_eleme...]
    gather x2 -> x4, local copies, waits for them, and re-layouts: 10.4 us -> 6.54 us  [relocate(): chosen = jnp.take(spread, pair_match, axis=0)]
  transfers between devices with their start and end apart: 7 -> 7, of which waited for: 2 -> 4; matrix products, arithmetic and copies ran while one was open for 19% -> 8% of each run, Pallas kernels for 0% -> 0%
where the time goes in v2:
time: 436 us; the launch traced here: 435 us
  blocking collectives  239 us (55%)
  waiting for transfers between devices  113 us (26%)
  matrix products  20.1 us (5%)
  starting transfers between devices  18.2 us (4%)
  other arithmetic  16.2 us (4%)
  between operations  15.9 us (4%)
  local copies, waits for them, and re-layouts  13.1 us (3%)
    all_to_all x3, blocking collectives, relocate(): lax.all_to_all(chosen, 'expert', split_axis=0, concat_axis=0, tiled=True)  105 us
    all_gather x1, blocking collectives, dense_gradient(): routing = lax.all_gather(routing, 'expert', axis=0, tiled=True)  83.7 us
    all_to_all x3, waiting for transfers between devices, relocate(): lax.all_to_all(pieces, 'expert', split_axis=0, concat_axis=0, tiled=True)  55.9 us
    all_to_all x1, blocking collectives, relocate(): lax.all_to_all(pieces, 'expert', split_axis=0, concat_axis=0, tiled=True)  40.2 us
    all_to_all x1, waiting for transfers between devices, relocate(): lax.all_to_all(chosen, 'expert', split_axis=0, concat_axis=0, tiled=True)  35 us
    all_gather x1, waiting for transfers between devices, dense_gradient(): lax.all_gather(jnp.stack((tokens, cotangent)), 'expert', axis=1, tiled=True)  22 us
    dot_general x1, matrix products, dense_gradient(): lax.dot_general(hidden, scaled, (((0,), (0,)), ((), ())), preferred_eleme...  20.1 us
    all_to_all x3, starting transfers between devices, relocate(): lax.all_to_all(pieces, 'expert', split_axis=0, concat_axis=0, tiled=True)  14.5 us
  transfers between devices with their start and end apart: 7, of which 4 were waited for; matrix products, arithmetic and copies ran while one was open for 8% of the time, Pallas kernels for 0%

profile of v2, /device:TPU:0, one launch (start us, length us, event | category | flops | bytes accessed | tf_op | source)
XLA Modules:
  0.0 435.4 jit_solution(3912501438321845362)
XLA Ops:
  7.2 1.3 copy.15
  9.5 6.4 %all-to-all-start.4 = ((bf16[8,256,192]{1,2,0:T(8,128)(2,1)}), bf16[8,256,192]{1,2,0:T(8,128)(2,1)S(1)}, u32[]{:S(2)}, u32[]{:S(2)}) async-start(bf16[8,256,192]{1,2,0:T(8,128)(2,1)} %copy.12), calls=%async_computation.4 | async-start | bytes 1572864 | tf_op jit(solution)/shard_map/all_to_all | solution.py:17
  16.0 20.9 %all-to-all-done.4 = bf16[8,256,192]{1,2,0:T(8,128)(2,1)S(1)} async-done(((bf16[8,256,192]{1,2,0:T(8,128)(2,1)}), bf16[8,256,192]{1,2,0:T(8,128)(2,1)S(1)}, u32[]{:S(2)}, u32[]{:S(2)}) %all-to-all-start.4) | async-done | bytes 786464 | tf_op jit(solution)/shard_map/all_to_all | solution.py:17
  37.6 23.4 %all_to_all.40 = bf16[8,256,192]{1,2,0:T(8,128)(2,1)S(1)} all-to-all(bf16[8,256,192]{1,2,0:T(8,128)(2,1)S(1)} %broadcast_select_fusion.3), channel_id=1, replica_groups=mesh['dp'=4,'expert'=8] {'expert'}, dimensions={0} | all-to-all | bytes 1572864 | tf_op jit(solution)/shard_map/all_to_all | solution.py:19
  64.2 40.2 %all_to_all.41 = f32[8,24,2048]{2,1,0:T(8,128)S(1)} all-to-all(f32[8,24,2048]{2,1,0:T(8,128)S(1)} %bitcast.43), channel_id=1, replica_groups=mesh['dp'=4,'expert'=8] {'expert'}, dimensions={0} | all-to-all | bytes 3145728 | tf_op jit(solution)/shard_map/all_to_all | solution.py:17
  104.4 3.7 all-to-all-start.2
  109.5 83.7 %all_gather.11 = f32[1024,8]{0,1:T(8,128)S(1)} all-gather(f32[128,8]{0,1:T(8,128)S(1)} %pad_maximum_fusion.1), channel_id=1, replica_groups=mesh['dp'=4,'expert'=8] {'expert'}, dimensions={0}, use_global_device_ids=true | all-gather | bytes 36864 | tf_op jit(solution)/shard_map/all_gather | solution.py:68
  193.3 22.0 %all-gather.3.cloned.1.call-done = bf16[2,1024,2048]{2,1,0:T(8,128)(2,1)} async-done(((bf16[2,128,2048]{2,1,0:T(8,128)(2,1)}), bf16[2,1024,2048]{2,1,0:T(8,128)(2,1)}) %all-gather.3.cloned.1.call-update) | async-done | bytes 8388624 | tf_op jit(solution)/shard_map/all_gather | solution.py:66
  215.2 20.1 %fusion.1 = f32[768,2048]{1,0:T(8,128)} fusion(bf16[2,1024,2048]{2,1,0:T(8,128)(2,1)} %all-gather.3.cloned.1.call-done, f32[1024]{0:T(1024)S(1)} %fusion.7, bf16[2048,768]{0,1:T(8,128)(2,1)} %all-gather.5.cloned.1.call-done), kind=kOutput, calls=%fused_computation.6 | convolution fusion | flops 6452674560 | bytes 17829888 | tf_op jit(solution)/shard_map/dot_general | solution.py:76
  235.4 1.1 copy-done.1
  236.5 4.5 %all-to-all-start.6 = ((f32[8,24,2048]{2,1,0:T(8,128)}), f32[8,24,2048]{2,1,0:T(8,128)}, u32[]{:S(2)}, u32[]{:S(2)}) async-start(f32[8,24,2048]{2,1,0:T(8,128)} %bitcast.45), calls=%async_computation.7 | async-start | bytes 3145728 | tf_op jit(solution)/shard_map/all_to_all | solution.py:17
  241.7 2.1 gather_fusion.2
  243.8 35.0 %all-to-all-done.6 = f32[8,24,2048]{2,1,0:T(8,128)} async-done(((f32[8,24,2048]{2,1,0:T(8,128)}), f32[8,24,2048]{2,1,0:T(8,128)}, u32[]{:S(2)}, u32[]{:S(2)}) %all-to-all-start.6) | async-done | bytes 1572896 | tf_op jit(solution)/shard_map/all_to_all | solution.py:17
  278.8 3.2 gather_fusion.3
  282.0 3.1 broadcast_select_fusion.1
  285.1 40.9 %all_to_all.42 = f32[8,24,2048]{2,1,0:T(8,128)} all-to-all(f32[8,24,2048]{2,1,0:T(8,128)S(1)} %get-tuple-element.10), channel_id=1, replica_groups=mesh['dp'=4,'expert'=8] {'expert'}, dimensions={0} | all-to-all | bytes 3145728 | tf_op jit(solution)/shard_map/all_to_all | solution.py:19
  326.0 40.2 %all_to_all.43 = f32[8,24,2048]{2,1,0:T(8,128)S(1)} all-to-all(f32[8,24,2048]{2,1,0:T(8,128)S(1)} %get-tuple-element.11), channel_id=1, replica_groups=mesh['dp'=4,'expert'=8] {'expert'}, dimensions={0} | all-to-all | bytes 3145728 | tf_op jit(solution)/shard_map/all_to_all | solution.py:19
  366.2 3.6 all-to-all-start.3
  371.2 1.3 broadcast_multiply_fusion
  372.5 35.0 %all-to-all-done.3 = f32[8,24,2048]{2,1,0:T(8,128)S(1)} async-done(((f32[8,24,2048]{2,1,0:T(8,128)}), f32[8,24,2048]{2,1,0:T(8,128)S(1)}, u32[]{:S(2)}, u32[]{:S(2)}) %all-to-all-start.3) | async-done | bytes 1572896 | tf_op jit(solution)/shard_map/all_to_all | solution.py:19
  407.6 1.3 broadcast_multiply_fusion.1
  408.9 5.0 %multiply_reduce_fusion = (f32[]{:T(128)}, f32[192,2048]{1,0:T(8,128)S(1)}, f32[192,2048]{1,0:T(8,128)}) fusion(f32[192,2048]{1,0:T(8,128)} %reduce-scatter.2.cloned.1.call-done, f32[8,24,2048]{2,1,0:T(8,128)} %broadcast_multiply_fusion, f32[8,24,2048]{2,1,0:T(8,128)} %broadcast_multiply_fusion.1), kind=kLoop, calls=%fused_computation.16 | loop fusion | flops 3538943 | bytes 7864324 | tf_op jit(solution)/shard_map/reduce_sum | solution.py:85
  413.8 10.5 %all-reduce = (f32[]{:T(128)}, f32[]{:T(128)}) all-reduce(f32[]{:T(128)} %multiply_reduce_fusion.1, f32[]{:T(128)} %get-tuple-element.6), channel_id=1, replica_groups=mesh['dp'=4,'expert'=8] {'dp'}, use_global_device_ids=true, to_apply=%region_1.3 | all-reduce | flops 2 | bytes 16 | tf_op jit(solution)/shard_map/psum | solution.py:85
  425.6 3.3 bitcast_subtract_fusion
  (40 shorter events, 7.8 us)
Async XLA Ops:
  8.5 7.4 %copy-start.8 = (s32[8]{0:T(128)S(1)}, s32[8]{0:T(128)}, u32[]{:S(2)}) copy-start(s32[8]{0:T(128)} %param.19) | copy-start | bytes 100
  9.5 27.3 %all-to-all-start.4 = ((bf16[8,256,192]{1,2,0:T(8,128)(2,1)}), bf16[8,256,192]{1,2,0:T(8,128)(2,1)S(1)}, u32[]{:S(2)}, u32[]{:S(2)}) async-start(bf16[8,256,192]{1,2,0:T(8,128)(2,1)} %copy.12), calls=%async_computation.4 | async-start | bytes 1572864 | tf_op jit(solution)/shard_map/all_to_all | solution.py:17
  15.9 177.3 %all-gather.5.cloned.1.call-start = ((), (), s32[]{:S(2)}) async-start(), calls=%async_computation.10 | async-start | bytes 3932160 | tf_op jit(solution)/shard_map/all_gather | solution.py:100
  61.0 1.2 copy-start.4
  61.0 1.5 copy-start.5
  62.0 153.3 %all-gather.3.cloned.1.call-start = ((), (), s32[]{:S(2)}) async-start(), calls=%async_computation.9 | async-start | bytes 9437184 | tf_op jit(solution)/shard_map/all_gather | solution.py:66
  62.4 1.8 copy-start.3
  104.4 5.0 %copy-start.6 = (s32[128,4]{0,1:T(4,128)S(1)}, s32[128,4]{0,1:T(4,128)}, u32[]{:S(2)}) copy-start(s32[128,4]{0,1:T(4,128)} %param.13) | copy-start | bytes 6148
  104.4 5.0 %copy-start.7 = (f32[128,4]{0,1:T(4,128)S(1)}, f32[128,4]{0,1:T(4,128)}, u32[]{:S(2)}) copy-start(f32[128,4]{0,1:T(4,128)} %param.14) | copy-start | bytes 6148
  104.4 130.9 %all-to-all-start.2 = ((f32[8,24,2048]{2,1,0:T(8,128)}), f32[8,24,2048]{2,1,0:T(8,128)S(1)}, u32[]{:S(2)}, u32[]{:S(2)}) async-start(f32[8,24,2048]{2,1,0:T(8,128)} %bitcast.44), calls=%async_computation.2 | async-start | bytes 3145728 | tf_op jit(solution)/shard_map/all_to_all | solution.py:17
  108.2 300.7 %reduce-scatter.2.cloned.1.call-start = ((), (), s32[]{:S(2)}) async-start(), calls=%async_computation.11 | async-start | bytes 7864320 | tf_op jit(solution)/shard_map/reduce_scatter | solution.py:105
  235.4 1.1 copy-start.1
  236.5 42.3 %all-to-all-start.6 = ((f32[8,24,2048]{2,1,0:T(8,128)}), f32[8,24,2048]{2,1,0:T(8,128)}, u32[]{:S(2)}, u32[]{:S(2)}) async-start(f32[8,24,2048]{2,1,0:T(8,128)} %bitcast.45), calls=%async_computation.7 | async-start | bytes 3145728 | tf_op jit(solution)/shard_map/all_to_all | solution.py:17
  366.2 41.3 %all-to-all-start.3 = ((f32[8,24,2048]{2,1,0:T(8,128)}), f32[8,24,2048]{2,1,0:T(8,128)S(1)}, u32[]{:S(2)}, u32[]{:S(2)}) async-start(f32[8,24,2048]{2,1,0:T(8,128)} %get-tuple-element.9), calls=%async_computation.3 | async-start | bytes 3145728 | tf_op jit(solution)/shard_map/all_to_all | solution.py:19
  369.8 1.4 copy-start
  413.8 15.1 %copy-start.2 = (f32[192,2048]{1,0:T(8,128)}, f32[192,2048]{1,0:T(8,128)S(1)}, u32[]{:S(2)}) copy-start(f32[192,2048]{1,0:T(8,128)S(1)} %get-tuple-element.7) | copy-start | bytes 4718596
Sparse Core Ops, SparseCore 0:
  62.1 42.7 all-gather.4
  107.1 108.1 all-gather.2
  235.5 69.0 reduce-scatter.1

commit v3 on v2

--- a/solution.py
+++ b/solution.py
@@ -9,6 +9,7 @@
 learn_rate = 0.05
 
 dense_rows_max = 2048
+exchange_group_max = 8
 
 
 def relocate(state, pair_match):
@@ -18,6 +19,32 @@
     chosen = jnp.take(spread, pair_match, axis=0)
     arrived = lax.all_to_all(chosen, "expert", split_axis=0, concat_axis=0, tiled=True)
     return arrived.reshape(state.shape)
+
+
+def perfect_matchings(members):
+    if not members:
+        return [()]
+    first, rest = members[0], members[1:]
+    found = []
+    for at, other in enumerate(rest):
+        for tail in perfect_matchings(rest[:at] + rest[at + 1 :]):
+            found.append(((first, other),) + tail)
+    return found
+
+
+def exchange(states, pair_match):
+    group_size = lax.axis_size("expert")
+    matchings = perfect_matchings(tuple(range(group_size)))
+    scale = [group_size**place for place in range(group_size)]
+    keys = [sum(scale[a] * b + scale[b] * a for a, b in pairs) for pairs in matchings]
+    key = jnp.sum(pair_match * jnp.array(scale, jnp.int32))
+    branch = jnp.argmax(jnp.array(keys, jnp.int32) == key).astype(jnp.int32)
+
+    def swap(pairs):
+        perm = [(a, b) for a, b in pairs] + [(b, a) for a, b in pairs]
+        return lambda values: tuple(lax.ppermute(value, "expert", perm) for value in values)
+
+    return lax.switch(branch, [swap(pairs) for pairs in matchings], tuple(states))
 
 
 def routed_gradient(tokens, cotangent, dest_ids, gate_probs, up_full):
@@ -93,10 +120,11 @@
 ):
     group_size = lax.axis_size("expert")
     partner = pair_match[lax.axis_index("expert")]
-    up_local = relocate(up_weight[0], pair_match)
-    weight = relocate(down_weight[0], pair_match)
-    moment_one = relocate(moment1[0], pair_match)
-    moment_two = relocate(moment2[0], pair_match)
+    states = (up_weight[0], down_weight[0], moment1[0], moment2[0])
+    if group_size <= exchange_group_max:
+        up_local, weight, moment_one, moment_two = exchange(states, pair_match)
+    else:
+        up_local, weight, moment_one, moment_two = (relocate(x, pair_match) for x in states)
     up_full = lax.all_gather(up_local, "dp", axis=1, tiled=True)
     if group_size * tokens.shape[0] <= dense_rows_max:
         partial = dense_gradient(tokens, cotangent, expert_ids, gate_probs, up_full, partner)

time: 436 us -> 412 us (0.945); the launches traced: 435 us -> 405 us
  blocking collectives: 239 us -> 23.9 us
  waiting for transfers between devices: 113 us -> 281 us
  loops' own time: 0 us -> 23.2 us
  local copies, waits for them, and re-layouts: 13.1 us -> 0.61 us
  starting transfers between devices: 18.2 us -> 24.4 us
    all_to_all x4 -> x0, blocking collectives: 145 us -> none  [the longest x3 105 us: relocate(): lax.all_to_all(chosen, 'expert', split_axis=0, concat_axis=0, tiled=True)]
    ppermute x0 -> x4, waiting for transfers between devices: none -> 103 us  [swap(): lax.ppermute(value, 'expert', perm)]
    all_to_all x4 -> x0, waiting for transfers between devices: 90.9 us -> none  [the longest x3 55.9 us: relocate(): lax.all_to_all(pieces, 'expert', split_axis=0, concat_axis=0, tiled=True)]
    all_gather x1, blocking collectives: 83.7 us -> 14.3 us  [dense_gradient(): routing = lax.all_gather(routing, 'expert', axis=0, tiled=True)]
    reduce_scatter x1, waiting for transfers between devices: 0.01 us -> 66.2 us  [local(): gradient = lax.psum_scatter(partial, 'dp', scatter_dimension=0, tiled=True)]
    all_gather x1, waiting for transfers between devices: 22 us -> 84.2 us  [dense_gradient(): lax.all_gather(jnp.stack((tokens, cotangent)), 'expert', axis=1, tiled=True)]
    all_gather x1, waiting for transfers between devices: 0.02 us -> 27.9 us  [local(): up_full = lax.all_gather(up_local, 'dp', axis=1, tiled=True)]
    ppermute x0 -> x4, starting transfers between devices: none -> 24.3 us  [swap(): lax.ppermute(value, 'expert', perm)]
  transfers between devices with their start and end apart: 7 -> 7, of which waited for: 4 -> 4; matrix products, arithmetic and copies ran while one was open for 8% -> 1% of each run, Pallas kernels for 0% -> 0%
where the time goes in v3:
time: 412 us; the launch traced here: 405 us
  waiting for transfers between devices  281 us (68%)
  starting transfers between devices  24.4 us (6%)
  blocking collectives  23.9 us (6%)
  loops' own time  23.2 us (6%)
  matrix products  20 us (5%)
  between operations  16.8 us (4%)
  other arithmetic  15.2 us (4%)
    ppermute x4, waiting for transfers between devices, swap(): lax.ppermute(value, 'expert', perm)  103 us
    all_gather x1, waiting for transfers between devices, dense_gradient(): lax.all_gather(jnp.stack((tokens, cotangent)), 'expert', axis=1, tiled=True)  84.2 us
    reduce_scatter x1, waiting for transfers between devices, local(): gradient = lax.psum_scatter(partial, 'dp', scatter_dimension=0, tiled=True)  66.2 us
    all_gather x1, waiting for transfers between devices, local(): up_full = lax.all_gather(up_local, 'dp', axis=1, tiled=True)  27.9 us
    ppermute x4, starting transfers between devices, swap(): lax.ppermute(value, 'expert', perm)  24.3 us
    another operation x1, loops' own time, exchange(): lax.switch(branch, [swap(pairs) for pairs in matchings], tuple(states))  23.2 us
    dot_general x1, matrix products, dense_gradient(): lax.dot_general(hidden, scaled, (((0,), (0,)), ((), ())), preferred_eleme...  20 us
    all_gather x1, blocking collectives, dense_gradient(): routing = lax.all_gather(routing, 'expert', axis=0, tiled=True)  14.3 us
  transfers between devices with their start and end apart: 7, of which 4 were waited for; matrix products, arithmetic and copies ran while one was open for 1% of the time, Pallas kernels for 0%

profile of v3, /device:TPU:0, one launch (start us, length us, event | category | flops | bytes accessed | tf_op | source)
XLA Modules:
  0.0 405.2 jit_solution(2822564870932152209)
XLA Ops:
  7.2 0.0 all-gather.5.cloned.1.call-start
  7.2 1.4 multiply_reduce_fusion.2
  8.6 2.0 compare_reduce_fusion
  11.2 150.2 %conditional.1 = (bf16[2048,192]{0,1:T(8,128)(2,1)}, f32[192,2048]{1,0:T(8,128)}, f32[192,2048]{1,0:T(8,128)}, f32[192,2048]{1,0:T(8,128)}) conditional(s32[]{:T(128)} %clamp.3, (bf16[2048,192]{0,1:T(8,128)(2,1)}, f32[192,2048]{1,0:T(8,128)}, f32[192,2048]{1,0:T(8,128)}, f32[192,2048]{1,0:T(8,128)}) %tuple.913, ...), branch_computations={%region_2.3_spmd, %region_3.4_spmd, %region_4.5_spmd, %region_5.6_... | conditional | bytes 22020288 | solution.py:47
  11.3 7.2 %collective-permute-start.97 = (f32[192,2048]{1,0:T(8,128)}, f32[192,2048]{1,0:T(8,128)}, u32[]{:S(2)}, u32[]{:S(2)}) collective-permute-start(f32[192,2048]{1,0:T(8,128)} %get-tuple-element.937), channel_id=1, source_target_pairs={{0,2},{1,6},{3,4},{5,7},{2,0},{6,1},{4,3},{7,5},{8,10},{9,14},{11,... | collective-permute-start | bytes 4718600 | tf_op jit(solution)/shard_map/cond/branch_24_fun/ppermute | solution.py:45
  18.4 5.7 %collective-permute-start.98 = (f32[192,2048]{1,0:T(8,128)}, f32[192,2048]{1,0:T(8,128)}, u32[]{:S(2)}, u32[]{:S(2)}) collective-permute-start(f32[192,2048]{1,0:T(8,128)} %get-tuple-element.938), channel_id=1, source_target_pairs={{0,2},{1,6},{3,4},{5,7},{2,0},{6,1},{4,3},{7,5},{8,10},{9,14},{11,... | collective-permute-start | bytes 4718600 | tf_op jit(solution)/shard_map/cond/branch_24_fun/ppermute | solution.py:45
  24.1 5.7 %collective-permute-start.99 = (f32[192,2048]{1,0:T(8,128)}, f32[192,2048]{1,0:T(8,128)}, u32[]{:S(2)}, u32[]{:S(2)}) collective-permute-start(f32[192,2048]{1,0:T(8,128)} %get-tuple-element.939), channel_id=1, source_target_pairs={{0,2},{1,6},{3,4},{5,7},{2,0},{6,1},{4,3},{7,5},{8,10},{9,14},{11,... | collective-permute-start | bytes 4718600 | tf_op jit(solution)/shard_map/cond/branch_24_fun/ppermute | solution.py:45
  29.9 5.7 %collective-permute-start.96 = (bf16[2048,192]{0,1:T(8,128)(2,1)}, bf16[2048,192]{0,1:T(8,128)(2,1)}, u32[]{:S(2)}, u32[]{:S(2)}) collective-permute-start(bf16[2048,192]{0,1:T(8,128)(2,1)} %get-tuple-element.936), channel_id=1, source_target_pairs={{0,2},{1,6},{3,4},{5,7},{2,0},{6,1},{4,3},{7,5},{8,10},{9,14},{11,... | collective-permute-start | bytes 2359304 | tf_op jit(solution)/shard_map/cond/branch_24_fun/ppermute | solution.py:45
  35.6 102.7 %collective-permute-done.96 = bf16[2048,192]{0,1:T(8,128)(2,1)} collective-permute-done((bf16[2048,192]{0,1:T(8,128)(2,1)}, bf16[2048,192]{0,1:T(8,128)(2,1)}, u32[]{:S(2)}, u32[]{:S(2)}) %collective-permute-start.96) | collective-permute-done | bytes 786464 | tf_op jit(solution)/shard_map/cond/branch_24_fun/ppermute | solution.py:45
  161.4 0.0 all-gather.5.cloned.1.call-update
  161.4 0.0 all-gather.3.cloned.1.call-start
  161.5 1.1 pad_maximum_fusion
  162.6 0.0 all-gather.3.cloned.1.call-update
  162.6 0.0 reduce-scatter.2.cloned.1.call-start
  162.7 0.6 dynamic_slice.3
  164.0 14.3 %all_gather.11 = f32[1024,8]{0,1:T(8,128)S(1)} all-gather(f32[128,8]{0,1:T(8,128)S(1)} %pad_maximum_fusion.1), channel_id=1, replica_groups=mesh['dp'=4,'expert'=8] {'expert'}, dimensions={0}, use_global_device_ids=true | all-gather | bytes 36864 | tf_op jit(solution)/shard_map/all_gather | solution.py:95
  178.3 27.9 %all-gather.5.cloned.1.call-done = bf16[2048,768]{0,1:T(8,128)(2,1)} async-done(((bf16[2048,192]{0,1:T(8,128)(2,1)}), bf16[2048,768]{0,1:T(8,128)(2,1)}) %all-gather.5.cloned.1.call-update) | async-done | bytes 3145744 | tf_op jit(solution)/shard_map/all_gather | solution.py:128
  206.2 84.2 %all-gather.3.cloned.1.call-done = bf16[2,1024,2048]{2,1,0:T(8,128)(2,1)} async-done(((bf16[2,128,2048]{2,1,0:T(8,128)(2,1)}), bf16[2,1024,2048]{2,1,0:T(8,128)(2,1)}) %all-gather.3.cloned.1.call-update) | async-done | bytes 8388624 | tf_op jit(solution)/shard_map/all_gather | solution.py:93
  290.5 20.0 %fusion.1 = f32[768,2048]{1,0:T(8,128)} fusion(bf16[2,1024,2048]{2,1,0:T(8,128)(2,1)} %all-gather.3.cloned.1.call-done, f32[1024]{0:T(1024)S(1)} %fusion.9, bf16[2048,768]{0,1:T(8,128)(2,1)} %all-gather.5.cloned.1.call-done), kind=kOutput, calls=%fused_computation.2 | convolution fusion | flops 6452674560 | bytes 17829888 | tf_op jit(solution)/shard_map/dot_general | solution.py:103
  310.6 2.4 multiply_reduce_fusion.1
  313.0 66.2 %reduce-scatter.2.cloned.1.call-done = f32[192,2048]{1,0:T(8,128)} async-done(((f32[768,2048]{1,0:T(8,128)}), f32[192,2048]{1,0:T(8,128)}) %reduce-scatter.2.cloned.1.call-update) | async-done | bytes 1572880 | tf_op jit(solution)/shard_map/reduce_scatter | solution.py:133
  379.2 5.6 %multiply_reduce_fusion = (f32[]{:T(128)}, f32[192,2048]{1,0:T(8,128)S(1)}, f32[1,192,2048]{2,1,0:T(8,128)}, f32[1,192,2048]{2,1,0:T(8,128)}) fusion(f32[192,2048]{1,0:T(8,128)} %reduce-scatter.2.cloned.1.call-done, f32[192,2048]{1,0:T(8,128)} %get-tuple-element.1272, f32[192,2048]{1,0:T(8,128)} %get-tuple-element.1270), kind=kLoop, calls=%fused_computation.11 | loop fusion | flops 4325375 | bytes 9437188 | tf_op jit(solution)/shard_map/reduce_sum | solution.py:112
  384.8 9.6 %all-reduce = (f32[]{:T(128)}, f32[]{:T(128)}) all-reduce(f32[]{:T(128)} %multiply_reduce_fusion.1, f32[]{:T(128)} %get-tuple-element.1275), channel_id=1, replica_groups=mesh['dp'=4,'expert'=8] {'dp'}, use_global_device_ids=true, to_apply=%region_108.109 | all-reduce | flops 2 | bytes 16 | tf_op jit(solution)/shard_map/psum | solution.py:112
  395.8 2.7 subtract_bitcast_fusion
  (17 shorter events, 0.1 us)
Async XLA Ops:
  7.2 154.3 %copy-start.1 = (bf16[128,2048]{1,0:T(8,128)(2,1)S(1)}, bf16[128,2048]{1,0:T(8,128)(2,1)}, u32[]{:S(2)}) copy-start(bf16[128,2048]{1,0:T(8,128)(2,1)} %param.116) | copy-start | bytes 1572868
  7.2 154.3 %copy-start = (bf16[128,2048]{1,0:T(8,128)(2,1)S(1)}, bf16[128,2048]{1,0:T(8,128)(2,1)}, u32[]{:S(2)}) copy-start(bf16[128,2048]{1,0:T(8,128)(2,1)} %param.117) | copy-start | bytes 1572868
  7.2 199.1 %all-gather.5.cloned.1.call-start = ((), (), s32[]{:S(2)}) async-start(), calls=%async_computation.2 | async-start | bytes 3932160 | tf_op jit(solution)/shard_map/all_gather | solution.py:128
  11.3 127.0 %collective-permute-start.97 = (f32[192,2048]{1,0:T(8,128)}, f32[192,2048]{1,0:T(8,128)}, u32[]{:S(2)}, u32[]{:S(2)}) collective-permute-start(f32[192,2048]{1,0:T(8,128)} %get-tuple-element.937), channel_id=1, source_target_pairs={{0,2},{1,6},{3,4},{5,7},{2,0},{6,1},{4,3},{7,5},{8,10},{9,14},{11,... | collective-permute-start | bytes 4718600 | tf_op jit(solution)/shard_map/cond/branch_24_fun/ppermute | solution.py:45
  18.4 119.9 %collective-permute-start.98 = (f32[192,2048]{1,0:T(8,128)}, f32[192,2048]{1,0:T(8,128)}, u32[]{:S(2)}, u32[]{:S(2)}) collective-permute-start(f32[192,2048]{1,0:T(8,128)} %get-tuple-element.938), channel_id=1, source_target_pairs={{0,2},{1,6},{3,4},{5,7},{2,0},{6,1},{4,3},{7,5},{8,10},{9,14},{11,... | collective-permute-start | bytes 4718600 | tf_op jit(solution)/shard_map/cond/branch_24_fun/ppermute | solution.py:45
  24.1 114.1 %collective-permute-start.99 = (f32[192,2048]{1,0:T(8,128)}, f32[192,2048]{1,0:T(8,128)}, u32[]{:S(2)}, u32[]{:S(2)}) collective-permute-start(f32[192,2048]{1,0:T(8,128)} %get-tuple-element.939), channel_id=1, source_target_pairs={{0,2},{1,6},{3,4},{5,7},{2,0},{6,1},{4,3},{7,5},{8,10},{9,14},{11,... | collective-permute-start | bytes 4718600 | tf_op jit(solution)/shard_map/cond/branch_24_fun/ppermute | solution.py:45
  29.9 108.4 %collective-permute-start.96 = (bf16[2048,192]{0,1:T(8,128)(2,1)}, bf16[2048,192]{0,1:T(8,128)(2,1)}, u32[]{:S(2)}, u32[]{:S(2)}) collective-permute-start(bf16[2048,192]{0,1:T(8,128)(2,1)} %get-tuple-element.936), channel_id=1, source_target_pairs={{0,2},{1,6},{3,4},{5,7},{2,0},{6,1},{4,3},{7,5},{8,10},{9,14},{11,... | collective-permute-start | bytes 2359304 | tf_op jit(solution)/shard_map/cond/branch_24_fun/ppermute | solution.py:45
  161.4 129.0 %all-gather.3.cloned.1.call-start = ((), (), s32[]{:S(2)}) async-start(), calls=%async_computation.1 | async-start | bytes 9437184 | tf_op jit(solution)/shard_map/all_gather | solution.py:93
  161.5 1.2 copy-start.4
  161.5 2.4 copy-start.2
  161.5 2.4 copy-start.3
  162.6 216.6 %reduce-scatter.2.cloned.1.call-start = ((), (), s32[]{:S(2)}) async-start(), calls=%async_computation.3 | async-start | bytes 7864320 | tf_op jit(solution)/shard_map/reduce_scatter | solution.py:133
Sparse Core Ops, SparseCore 0:
  161.6 44.6 all-gather.4
  208.4 82.0 all-gather.2
  310.7 68.5 reduce-scatter.1

commit v4 on v3

--- a/solution.py
+++ b/solution.py
@@ -88,9 +88,11 @@
     )
 
 
-def dense_gradient(tokens, cotangent, expert_ids, gate_probs, up_full, expert):
+def dense_gradient(tokens, cotangent, expert_ids, gate_probs, up_local, expert):
     top_count = expert_ids.shape[1]
     rows = lax.all_gather(jnp.stack((tokens, cotangent)), "expert", axis=1, tiled=True)
+    rows, up_local = lax.optimization_barrier((rows, up_local))
+    up_full = lax.all_gather(up_local, "dp", axis=1, tiled=True)
     routing = jnp.concatenate((gate_probs, expert_ids.astype(jnp.float32)), axis=1)
     routing = lax.all_gather(routing, "expert", axis=0, tiled=True)
     all_gates, all_ids = routing[:, :top_count], routing[:, top_count:]
@@ -120,15 +122,19 @@
 ):
     group_size = lax.axis_size("expert")
     partner = pair_match[lax.axis_index("expert")]
-    states = (up_weight[0], down_weight[0], moment1[0], moment2[0])
+    states = (down_weight[0], moment1[0], moment2[0])
     if group_size <= exchange_group_max:
-        up_local, weight, moment_one, moment_two = exchange(states, pair_match)
+        up_wide = up_weight[0].astype(jnp.float32).reshape(states[0].shape)
+        (swapped,) = exchange((jnp.stack((up_wide,) + states),), pair_match)
+        up_local = swapped[0].reshape(up_weight.shape[1:]).astype(jnp.bfloat16)
+        weight, moment_one, moment_two = swapped[1], swapped[2], swapped[3]
     else:
-        up_local, weight, moment_one, moment_two = (relocate(x, pair_match) for x in states)
-    up_full = lax.all_gather(up_local, "dp", axis=1, tiled=True)
+        up_local = relocate(up_weight[0], pair_match)
+        weight, moment_one, moment_two = (relocate(x, pair_match) for x in states)
     if group_size * tokens.shape[0] <= dense_rows_max:
-        partial = dense_gradient(tokens, cotangent, expert_ids, gate_probs, up_full, partner)
+        partial = dense_gradient(tokens, cotangent, expert_ids, gate_probs, up_local, partner)
     else:
+        up_full = lax.all_gather(up_local, "dp", axis=1, tiled=True)
         partial = routed_gradient(tokens, cotangent, pair_match[expert_ids], gate_probs, up_full)
     gradient = lax.psum_scatter(partial, "dp", scatter_dimension=0, tiled=True)
     renewed, first, second = lamb_step(weight, moment_one, moment_two, gradient)

time: 412 us -> 392 us (0.951); the launches traced: 405 us -> 391 us
  loops' own time: 23.2 us -> 0.06 us
  waiting for transfers between devices: 281 us -> 298 us
  starting transfers between devices: 24.4 us -> 7.58 us
  local copies, waits for them, and re-layouts: 0.61 us -> 8.69 us
    ppermute x4 -> x1, waiting for transfers between devices: 103 us -> 202 us  [swap(): lax.ppermute(value, 'expert', perm)]
    all_gather x1, waiting for transfers between devices: 84.2 us -> 0.02 us  [dense_gradient(): lax.all_gather(jnp.stack((tokens, cotangent)), 'expert', axis=1, tiled=True)]
    another operation x1, loops' own time: 23.2 us -> 0.06 us  [exchange(): lax.switch(branch, [swap(pairs) for pairs in matchings], tuple(states))]
    ppermute x4 -> x1, starting transfers between devices: 24.3 us -> 7.46 us  [swap(): lax.ppermute(value, 'expert', perm)]
    reduce_sum x2 -> x0, other arithmetic: 8.02 us -> none  [the longest x1 5.57 us: lamb_step(): jnp.sum(update * update)]
    broadcast_in_dim x1 -> x2, other arithmetic: 2.74 us -> 9.07 us  [local(): return (renewed[None], first[None], second[None])]
    convert_element_type x0 -> x3, local copies, waits for them, and re-layouts: none -> 5.33 us  [the longest x2 3.76 us: local(): up_wide = up_weight[0].astype(jnp.float32).reshape(states[0].shape)]
  transfers between devices with their start and end apart: 7 -> 4, of which waited for: 4 -> 3; matrix products, arithmetic and copies ran while one was open for 1% -> 3% of each run, Pallas kernels for 0% -> 0%
where the time goes in v4:
time: 392 us; the launch traced here: 391 us
  waiting for transfers between devices  298 us (76%)
  blocking collectives  23.6 us (6%)
  matrix products  20 us (5%)
  between operations  16.5 us (4%)
  other arithmetic  16.4 us (4%)
  local copies, waits for them, and re-layouts  8.69 us (2%)
  starting transfers between devices  7.58 us (2%)
    ppermute x1, waiting for transfers between devices, swap(): lax.ppermute(value, 'expert', perm)  202 us
    reduce_scatter x1, waiting for transfers between devices, local(): gradient = lax.psum_scatter(partial, 'dp', scatter_dimension=0, tiled=True)  70.2 us
    all_gather x1, waiting for transfers between devices, dense_gradient(): up_full = lax.all_gather(up_local, 'dp', axis=1, tiled=True)  26.7 us
    dot_general x1, matrix products, dense_gradient(): lax.dot_general(hidden, scaled, (((0,), (0,)), ((), ())), preferred_eleme...  20 us
    all_gather x1, blocking collectives, dense_gradient(): routing = lax.all_gather(routing, 'expert', axis=0, tiled=True)  14.1 us
    psum x1, blocking collectives, lamb_step(): lax.psum((jnp.sum(weight * weight), jnp.sum(update * update)), 'dp')  9.54 us
    broadcast_in_dim x2, other arithmetic, local(): return (renewed[None], first[None], second[None])  9.07 us
  transfers between devices with their start and end apart: 4, of which 3 were waited for; matrix products, arithmetic and copies ran while one was open for 3% of the time, Pallas kernels for 0%

profile of v4, /device:TPU:0, one launch (start us, length us, event | category | flops | bytes accessed | tf_op | source)
XLA Modules:
  0.0 391.4 jit_solution(1382776927174929950)
XLA Ops:
  7.2 0.0 all-gather.3.cloned.1.call-start
  7.2 2.3 pad_maximum_fusion.1
  9.5 0.0 all-gather.5.cloned.1.call-start
  9.6 1.4 copy.16
  11.0 2.3 reshape.27
  13.4 0.6 multiply_reduce_fusion.2
  14.0 1.4 compare_reduce_fusion
  16.0 3.1 pad_maximum_fusion
  19.1 209.0 %conditional.1 = (f32[4,192,2048]{2,1,0:T(8,128)}) conditional(s32[]{:T(128)} %clamp.3, f32[4,192,2048]{2,1,0:T(8,128)S(1)} %pad_maximum_fusion, f32[4,192,2048]{2,1,0:T(8,128)S(1)} %pad_maximum_fusion, f32[4,192,2048]{2,1,0:T(8,128)S(1)} %pad_maximum_fusion, f32[4,192,2048]{2,1,0:T(8,128)S(1)} %pad_maximum_fusion, ...), branch_computations={%region_2.3_spmd, %region_3.4_spmd, %region_4.5_spmd, %region_5.6_... | conditional | bytes 25165872 | solution.py:47
  19.2 7.5 %collective-permute-start.77 = (f32[4,192,2048]{2,1,0:T(8,128)S(1)}, f32[4,192,2048]{2,1,0:T(8,128)}, u32[]{:S(2)}, u32[]{:S(2)}) collective-permute-start(f32[4,192,2048]{2,1,0:T(8,128)S(1)} %param.77), channel_id=1, source_target_pairs={{0,6},{1,2},{3,7},{4,5},{6,0},{2,1},{7,3},{5,4},{8,14},{9,10},{11,... | collective-permute-start | bytes 18874376 | tf_op jit(solution)/shard_map/cond/branch_77_fun/ppermute | solution.py:45
  26.6 201.5 %collective-permute-done.77 = f32[4,192,2048]{2,1,0:T(8,128)} collective-permute-done((f32[4,192,2048]{2,1,0:T(8,128)S(1)}, f32[4,192,2048]{2,1,0:T(8,128)}, u32[]{:S(2)}, u32[]{:S(2)}) %collective-permute-start.77) | collective-permute-done | bytes 6291488 | tf_op jit(solution)/shard_map/cond/branch_77_fun/ppermute | solution.py:45
  228.1 1.5 slice.81
  229.6 1.6 convert_element_type.40
  231.2 0.0 all-gather.3.cloned.1.call-done
  231.3 1.2 copy.17
  232.5 0.0 reduce-scatter.2.cloned.1.call-start
  232.6 0.6 dynamic_slice.3
  233.8 14.1 %all_gather.11 = f32[1024,8]{0,1:T(8,128)S(1)} all-gather(f32[128,8]{0,1:T(8,128)S(1)} %pad_maximum_fusion.2), channel_id=1, replica_groups=mesh['dp'=4,'expert'=8] {'expert'}, dimensions={0}, use_global_device_ids=true | all-gather | bytes 36864 | tf_op jit(solution)/shard_map/all_gather | solution.py:97
  248.0 26.7 %all-gather.5.cloned.1.call-done = bf16[2048,768]{0,1:T(8,128)(2,1)} async-done(((bf16[2048,192]{0,1:T(8,128)(2,1)}), bf16[2048,768]{0,1:T(8,128)(2,1)}) %all-gather.5.cloned.1.call-update) | async-done | bytes 3145744 | tf_op jit(solution)/shard_map/all_gather | solution.py:95
  274.7 20.0 %fusion.1 = f32[768,2048]{1,0:T(8,128)} fusion(bf16[2,1024,2048]{2,1,0:T(8,128)(2,1)} %all-gather.3.cloned.1.call-done, f32[1024]{0:T(1024)S(1)} %fusion.20, bf16[2048,768]{0,1:T(8,128)(2,1)} %all-gather.5.cloned.1.call-done), kind=kOutput, calls=%fused_computation.3 | convolution fusion | flops 6452674560 | bytes 17829888 | tf_op jit(solution)/shard_map/dot_general | solution.py:105
  294.7 70.2 %reduce-scatter.2.cloned.1.call-done = f32[192,2048]{1,0:T(8,128)} async-done(((f32[768,2048]{1,0:T(8,128)}), f32[192,2048]{1,0:T(8,128)}) %reduce-scatter.2.cloned.1.call-update) | async-done | bytes 1572880 | tf_op jit(solution)/shard_map/reduce_scatter | solution.py:139
  364.9 6.3 %fusion.19 = (f32[1,192,2048]{2,1,0:T(8,128)}, f32[1,192,2048]{2,1,0:T(8,128)}, f32[]{:T(128)}, f32[192,2048]{1,0:T(8,128)S(1)}, f32[]{:T(128)}) fusion(f32[192,2048]{1,0:T(8,128)} %reduce-scatter.2.cloned.1.call-done, f32[4,192,2048]{2,1,0:T(8,128)} %get-tuple-element.229), kind=kLoop, calls=%fused_computation.27 | loop fusion | flops 5111806 | bytes 11010056 | tf_op jit(solution)/shard_map/broadcast_in_dim | solution.py:141
  371.2 9.5 %all-reduce = (f32[]{:T(128)}, f32[]{:T(128)}) all-reduce(f32[]{:T(128)} %get-tuple-element.228, f32[]{:T(128)} %get-tuple-element.226), channel_id=1, replica_groups=mesh['dp'=4,'expert'=8] {'dp'}, use_global_device_ids=true, to_apply=%region_108.109 | all-reduce | flops 2 | bytes 16 | tf_op jit(solution)/shard_map/psum | solution.py:114
  382.1 2.7 subtract_bitcast_fusion
  (16 shorter events, 0.1 us)
Async XLA Ops:
  7.2 6.2 %copy-start.4 = (s32[8]{0:T(128)S(1)}, s32[8]{0:T(128)}, u32[]{:S(2)}) copy-start(s32[8]{0:T(128)} %constant.37.clone) | copy-start | bytes 100
  7.2 6.8 %copy-start.2 = (s32[105]{0:T(128)S(1)}, s32[105]{0:T(128)}, u32[]{:S(2)}) copy-start(s32[105]{0:T(128)} %constant.38.clone) | copy-start | bytes 1264
  7.2 6.2 %copy-start.3 = (s32[8]{0:T(128)S(1)}, s32[8]{0:T(128)}, u32[]{:S(2)}) copy-start(s32[8]{0:T(128)} %param.124) | copy-start | bytes 100
  7.2 224.0 %all-gather.3.cloned.1.call-start = ((), (), s32[]{:S(2)}) async-start(), calls=%async_computation.1 | async-start | bytes 9437184 | tf_op jit(solution)/shard_map/all_gather | solution.py:93
  9.5 265.1 %all-gather.5.cloned.1.call-start = ((), (), s32[]{:S(2)}) async-start(), calls=%async_computation.2 | async-start | bytes 3932160 | tf_op jit(solution)/shard_map/all_gather | solution.py:95
  16.0 217.8 %copy-start = (s32[128,4]{0,1:T(4,128)S(1)}, s32[128,4]{0,1:T(4,128)}, u32[]{:S(2)}) copy-start(s32[128,4]{0,1:T(4,128)} %param.118) | copy-start | bytes 6148
  16.0 217.8 %copy-start.1 = (f32[128,4]{0,1:T(4,128)S(1)}, f32[128,4]{0,1:T(4,128)}, u32[]{:S(2)}) copy-start(f32[128,4]{0,1:T(4,128)} %param.119) | copy-start | bytes 6148
  19.2 209.0 %collective-permute-start.77 = (f32[4,192,2048]{2,1,0:T(8,128)S(1)}, f32[4,192,2048]{2,1,0:T(8,128)}, u32[]{:S(2)}, u32[]{:S(2)}) collective-permute-start(f32[4,192,2048]{2,1,0:T(8,128)S(1)} %param.77), channel_id=1, source_target_pairs={{0,6},{1,2},{3,7},{4,5},{6,0},{2,1},{7,3},{5,4},{8,14},{9,10},{11,... | collective-permute-start | bytes 18874376 | tf_op jit(solution)/shard_map/cond/branch_77_fun/ppermute | solution.py:45
  232.5 132.4 %reduce-scatter.2.cloned.1.call-start = ((), (), s32[]{:S(2)}) async-start(), calls=%async_computation.3 | async-start | bytes 7864320 | tf_op jit(solution)/shard_map/reduce_scatter | solution.py:139
Sparse Core Ops, SparseCore 0:
  10.2 145.6 all-gather.2
  232.6 41.9 all-gather.4
  294.8 70.0 reduce-scatter.1
